TPU v7x, 32 devices: a whole 2x2x4 slice. The times are simulated.
32 devices in a mesh: leaf: 4 (over y, x), src: 8 (over z, core).
Axes of the slice: x: 2, y: 2, z: 4, core: 2. Of those that a mesh axis runs over, the one named last changes fastest.
Arguments:
- src_cells: int32 [1024], P('src'), may hold values from 0 to 2047
- rec_cells: int32 [512], P('leaf'), may hold values from 0 to 511
- residual: float32 [1024, 512], P('src', 'leaf'), may hold values from -6 to 6
- pattern: int32 [12, 2], P('leaf'), may hold values 0 or 1
- leaf_lower: bfloat16 [2048, 512], P('leaf'), may hold values from -0.1875 to 0.1875
- leaf_upper: bfloat16 [2048, 512], P('leaf'), may hold values from -0.1875 to 0.1875
- leaf_inv: bfloat16 [16, 128, 128], P('leaf'), may hold values from -0.5 to 0.5
- anc_lower: bfloat16 [1024, 512], P('leaf'), may hold values from -0.125 to 0.125
- anc_upper: bfloat16 [2048, 256], P('leaf'), may hold values from -0.375 to 0.375
- sep_inv: bfloat16 [8, 128, 128], P('leaf'), may hold values from -0.5 to 0.5
- sep_lower: bfloat16 [8, 256, 128], P('leaf'), may hold values from -0.25 to 0.25
- sep_upper: bfloat16 [8, 128, 256], P('leaf'), may hold values from -0.375 to 0.375
Outputs:
- forward_field: float32 [1024, 2048], P('src', 'leaf')
- adjoint_field: float32 [1024, 2048], P('src', 'leaf')
- gradient: float32 [2048], P(('leaf', 'src'))
Inputs may be any that keep to these rules, and one draw needn't show every extreme that they name: src_cells holds 512 d + c for a source in interior cell c of subdomain d. rec_cells holds a receiver's cell within the subdomain of its block of 128 entries.
All inputs are finite; a program needn't handle non-finite values. No bound on the sum of `pattern` on one device may be relied on, other than what follows from the above.
Results may differ from a plain program's by a relative error of at most 0.0068.
Values may be sent and summed in bfloat16 or wider, within the bound.
No kernel may reach another device: no remote copies, remote signals or barrier semaphores. Data moves between devices by JAX's collectives and lax.ppermute only.
A program may use at most 64 MiB of HBM per device.

v0:
```python
import math
import jax
import jax.numpy as jnp
from jax import lax
from jax.sharding import PartitionSpec as P


def across(former, latter):
    return lax.dot_general(
        former, latter, (((1,), (1,)), ((), ())), preferred_element_type=jnp.float32
    )


def plain_dot(former, latter):
    return jnp.dot(former, latter, preferred_element_type=jnp.float32)


def as_half(values):
    return values.astype(jnp.bfloat16)


def lower_solve(right_side, lower, block_size, block_count):
    solved = []
    for index in range(block_count):
        segment = right_side[:, index * block_size : (index + 1) * block_size]
        if index:
            earlier = as_half(jnp.concatenate(solved, axis=1))
            segment = segment - across(
                earlier, lower[index * block_size : (index + 1) * block_size, : index * block_size]
            )
        solved.append(segment)
    return jnp.concatenate(solved, axis=1)


def upper_solve(right_side, upper, inverse, block_size, block_count):
    behind = []
    for index in reversed(range(block_count)):
        segment = right_side[:, index * block_size : (index + 1) * block_size]
        if behind:
            segment = segment - across(
                as_half(jnp.concatenate(behind, axis=1)),
                upper[index * block_size : (index + 1) * block_size, (index + 1) * block_size :],
            )
        behind.insert(0, across(as_half(segment), inverse[index]))
    return jnp.concatenate(behind, axis=1)


def upper_t_solve(right_side, upper, inverse, block_size, block_count):
    solved = []
    for index in range(block_count):
        segment = right_side[:, index * block_size : (index + 1) * block_size]
        if index:
            earlier = as_half(jnp.concatenate(solved, axis=1))
            segment = segment - plain_dot(
                earlier, upper[: index * block_size, index * block_size : (index + 1) * block_size]
            )
        solved.append(plain_dot(as_half(segment), inverse[index]))
    return jnp.concatenate(solved, axis=1)


def lower_t_solve(right_side, lower, block_size, block_count):
    behind = []
    for index in reversed(range(block_count)):
        segment = right_side[:, index * block_size : (index + 1) * block_size]
        if behind:
            segment = segment - plain_dot(
                as_half(jnp.concatenate(behind, axis=1)),
                lower[(index + 1) * block_size :, index * block_size : (index + 1) * block_size],
            )
        behind.insert(0, segment)
    return jnp.concatenate(behind, axis=1)


def climb(starts, handlers, levels, block_size, device):
    contributions = list(starts)
    results = [[] for member in starts]
    for height in range(1, levels + 1):
        lowest = (height - 1) * block_size
        piece = jnp.stack([summed[:, lowest : lowest + block_size] for summed in contributions])
        gathered = lax.all_gather(piece[None], "leaf", axis=0, tiled=True)
        first = device >> height << height
        total = jnp.sum(lax.dynamic_slice_in_dim(gathered, first, 1 << height, 0), axis=0)
        owner = device % (1 << height) == 0
        member = 0
        node_value, coupling = handlers[member](height, total[member])
        results[member].append(node_value)
        contributions[member] = contributions[member] + jnp.where(
            owner, coupling, jnp.zeros_like(coupling)
        )
    return results


def descend(node_values, handlers, levels, block_size, device, sources):
    known = [jnp.zeros((sources, levels * block_size), jnp.float32) for member in node_values]
    for height in range(levels, 0, -1):
        outgoing = jnp.stack([as_half(handlers[0](height, known[0], node_values[0][height - 1]))])
        gathered = lax.all_gather(outgoing[None], "leaf", axis=0, tiled=True)
        owner_index = device >> height << height
        piece = lax.dynamic_index_in_dim(gathered, owner_index, 0, keepdims=False).astype(
            jnp.float32
        )
        known = [lax.dynamic_update_slice_in_dim(known[0], piece[0], (height - 1) * block_size, 1)]
    return known


def shards(
    src_cells,
    rec_cells,
    residual,
    pattern,
    leaf_lower,
    leaf_upper,
    leaf_inv,
    anc_lower,
    anc_upper,
    sep_inv,
    sep_lower,
    sep_upper,
):
    levels = lax.axis_size("leaf").bit_length() - 1
    device = lax.axis_index("leaf")
    block_size = leaf_inv.shape[1]
    block_count = leaf_inv.shape[0]
    cell_count = leaf_lower.shape[1]
    source_count = src_cells.shape[0]
    factor = 1.0 / math.sqrt(source_count * lax.axis_size("src"))
    present = pattern.astype(jnp.float32)

    def level_mask(height):
        level_row = present[height] * (jnp.arange(1, levels + 1) > height).astype(jnp.float32)
        return jnp.repeat(level_row, block_size)

    columns = lax.broadcasted_iota(jnp.int32, (source_count, cell_count), 1)
    forcing = (src_cells[:, None] - device * cell_count == columns).astype(jnp.float32)
    receiver_hits = (
        rec_cells[:, None] == lax.broadcasted_iota(jnp.int32, (rec_cells.shape[0], cell_count), 1)
    ).astype(jnp.float32)
    adjoint_rhs = jnp.dot(residual, receiver_hits, precision=lax.Precision.HIGHEST)

    def forward_up(height, summed):
        node_value = -summed
        return (node_value, across(as_half(node_value), sep_lower[height - 1]) * level_mask(height))

    def adjoint_up(height, summed):
        node_value = plain_dot(as_half(-summed), sep_inv[height - 1])
        return (
            node_value,
            plain_dot(as_half(node_value), sep_upper[height - 1]) * level_mask(height),
        )

    def forward_down(height, above, node_value):
        right_side = node_value - across(as_half(above * level_mask(height)), sep_upper[height - 1])
        return across(as_half(right_side), sep_inv[height - 1])

    def adjoint_down(height, above, node_value):
        return node_value - plain_dot(as_half(above * level_mask(height)), sep_lower[height - 1])

    base_mask = level_mask(0)
    y_leaf = lower_solve(forcing, leaf_lower, block_size, block_count)
    forward_start = across(as_half(y_leaf), anc_lower) * base_mask
    z_leaf = upper_t_solve(adjoint_rhs, leaf_upper, leaf_inv, block_size, block_count)
    adjoint_start = plain_dot(as_half(z_leaf), anc_upper) * base_mask
    forward_values = climb([forward_start], [forward_up], levels, block_size, device)
    forward_above = descend(
        forward_values, [forward_down], levels, block_size, device, source_count
    )[0]
    adjoint_values = climb([adjoint_start], [adjoint_up], levels, block_size, device)
    adjoint_above = descend(
        adjoint_values, [adjoint_down], levels, block_size, device, source_count
    )[0]
    forward_remain = y_leaf - across(as_half(forward_above * base_mask), anc_upper)
    forward_field = upper_solve(forward_remain, leaf_upper, leaf_inv, block_size, block_count)
    adjoint_remain = z_leaf - plain_dot(as_half(adjoint_above * base_mask), anc_lower)
    adjoint_field = lower_t_solve(adjoint_remain, leaf_lower, block_size, block_count)
    partial_gradient = jnp.sum(forward_field * adjoint_field, axis=0)
    gradient = lax.psum_scatter(partial_gradient, "src", scatter_dimension=0, tiled=True) * factor
    return (forward_field, adjoint_field, gradient)


def solution(mesh):
    in_specs = (
        P("src"),
        P("leaf"),
        P("src", "leaf"),
        P("leaf", None),
        P("leaf", None),
        P("leaf", None),
        P("leaf", None, None),
        P("leaf", None),
        P("leaf", None),
        P("leaf", None, None),
        P("leaf", None, None),
        P("leaf", None, None),
    )
    out_specs = (P("src", "leaf"), P("src", "leaf"), P(("leaf", "src")))
    return jax.shard_map(shards, mesh=mesh, in_specs=in_specs, out_specs=out_specs, check_vma=False)
```

profile of v0, /device:TPU:0, one launch (start us, length us, event | category | flops | bytes accessed | tf_op | source)
XLA Modules:
  0.0 98.7 jit_solution(13294854775724279794)
XLA Ops:
  0.6 0.0 copy-start
  0.6 0.0 copy-start.7
  0.7 0.7 broadcast_subtract_fusion
  1.4 0.9 fusion.189
  2.3 0.0 copy-done.7
  2.4 0.1 fusion.190
  2.5 0.0 copy-start.5
  2.5 0.2 convolution_subtract_fusion.5
  2.7 0.0 copy-start.9
  2.7 0.7 copy-done.9
  3.4 0.2 slice_reduce_fusion
  3.6 0.1 broadcast_bitcast_fusion.1
  3.7 0.0 copy-done.5
  3.7 0.2 convolution_multiply_fusion.1
  3.9 0.0 copy-start.6
  4.0 10.6 %all-gather = f32[512,128]{1,0:T(8,128)S(1)} all-gather(f32[128,128]{1,0:T(8,128)S(1)} %slice.198), channel_id=2, replica_groups=mesh['leaf'=4,'src'=8] {'leaf'}, dimensions={0}, use_global_device_ids=true | all-gather | bytes 327680 | tf_op jit(solution)/shard_map/all_gather | solution.py:80
  14.5 0.0 copy-done.8
  14.6 0.0 copy-start.3
  14.6 0.4 convolution_bitcast_fusion
  15.0 0.5 copy-done.3
  15.5 0.2 fusion.180
  15.7 0.3 fusion.181
  16.0 0.4 fusion.184
  16.4 0.4 fusion.13
  16.8 0.0 copy-done
  16.8 0.2 convolution_multiply_fusion
  17.0 9.0 %all-gather.4 = f32[512,128]{1,0:T(8,128)S(1)} all-gather(f32[128,128]{1,0:T(8,128)S(1)} %slice.210), channel_id=6, replica_groups=mesh['leaf'=4,'src'=8] {'leaf'}, dimensions={0}, use_global_device_ids=true | all-gather | bytes 327680 | tf_op jit(solution)/shard_map/all_gather | solution.py:80
  26.0 0.0 copy-start.2
  26.0 0.8 copy-done.4
  26.8 0.1 fusion.121
  27.0 0.0 copy-done.2
  27.0 0.0 copy-start.1
  27.0 0.1 fusion.91
  27.1 0.8 copy-done.1
  27.9 0.2 fusion.98
  28.1 0.1 broadcast_bitcast_fusion
  28.2 8.1 %all-gather.1 = f32[512,128]{1,0:T(8,128)S(1)} all-gather(f32[128,128]{1,0:T(8,128)S(1)} %get-tuple-element.16), channel_id=3, replica_groups=mesh['leaf'=4,'src'=8] {'leaf'}, dimensions={0}, use_global_device_ids=true | all-gather | bytes 327680 | tf_op jit(solution)/shard_map/all_gather | solution.py:80
  36.3 0.1 broadcast_bitcast_fusion.2
  36.4 0.3 convolution_convert_fusion.1
  36.6 8.7 %all-gather.2 = bf16[512,128]{1,0:T(8,128)(2,1)S(1)} all-gather(bf16[128,128]{1,0:T(8,128)(2,1)S(1)} %convolution_convert_fusion.1), channel_id=4, replica_groups=mesh['leaf'=4,'src'=8] {'leaf'}, dimensions={0}, use_global_device_ids=true | all-gather | bytes 163840 | tf_op jit(solution)/shard_map/all_gather | solution.py:97
  45.4 0.3 convolution_convert_fusion
  45.7 7.3 %all-gather.3 = bf16[512,128]{1,0:T(8,128)(2,1)S(1)} all-gather(bf16[128,128]{1,0:T(8,128)(2,1)S(1)} %convolution_convert_fusion), channel_id=5, replica_groups=mesh['leaf'=4,'src'=8] {'leaf'}, dimensions={0}, use_global_device_ids=true | all-gather | bytes 163840 | tf_op jit(solution)/shard_map/all_gather | solution.py:97
  53.0 0.2 convolution_subtract_fusion.1
  53.2 0.1 fusion.193
  53.3 0.3 fusion.194
  53.6 0.3 fusion.197
  53.9 0.3 fusion.10
  54.2 9.2 %all-gather.5 = f32[512,128]{1,0:T(8,128)S(1)} all-gather(f32[128,128]{1,0:T(8,128)S(1)} %get-tuple-element.15), channel_id=7, replica_groups=mesh['leaf'=4,'src'=8] {'leaf'}, dimensions={0}, use_global_device_ids=true | all-gather | bytes 327680 | tf_op jit(solution)/shard_map/all_gather | solution.py:80
  63.5 0.1 fusion.122
  63.6 0.2 fusion.5
  63.7 7.3 %all-gather.6 = bf16[512,128]{1,0:T(8,128)(2,1)S(1)} all-gather(bf16[128,128]{1,0:T(8,128)(2,1)S(1)} %fusion.5), channel_id=8, replica_groups=mesh['leaf'=4,'src'=8] {'leaf'}, dimensions={0}, use_global_device_ids=true | all-gather | bytes 163840 | tf_op jit(solution)/shard_map/all_gather | solution.py:97
  71.1 0.1 fusion.6
  71.2 8.6 %all-gather.7 = bf16[512,128]{1,0:T(8,128)(2,1)S(1)} all-gather(bf16[128,128]{1,0:T(8,128)(2,1)S(1)} %fusion.6), channel_id=9, replica_groups=mesh['leaf'=4,'src'=8] {'leaf'}, dimensions={0}, use_global_device_ids=true | all-gather | bytes 163840 | tf_op jit(solution)/shard_map/all_gather | solution.py:97
  79.9 0.3 convolution_subtract_fusion
  80.1 0.2 fusion.191
  80.4 0.2 fusion.192
  80.6 0.2 convolution_subtract_fusion.8
  80.8 0.1 multiply_reduce_fusion
  81.0 0.8 copy.21
  81.8 0.8 copy.22
  82.7 13.6 %all-reduce.2 = f32[512]{0:T(512)S(1)} all-reduce(f32[512]{0:T(512)S(1)} %get-tuple-element.12), channel_id=10, replica_groups=mesh['leaf'=4,'src'=8] {'src'}, use_global_device_ids=true, to_apply=%region_5.6.clone | all-reduce | flops 512 | bytes 4096
  96.3 0.7 copy-done.11
  96.9 0.6 dynamic-slice
  98.1 0.6 dynamic-slice_multiply_fusion
  (26 shorter events, 0.2 us)
Async XLA Ops:
  0.6 16.1 %copy-start = (bf16[512,256]{1,0:T(8,128)(2,1)S(1)}, bf16[512,256]{1,0:T(8,128)(2,1)}, u32[]{:S(2)}) copy-start(bf16[512,256]{1,0:T(8,128)(2,1)} %param.20) | copy-start | bytes 786436
  0.6 1.7 %copy-start.7 = (bf16[512,512]{1,0:T(8,128)(2,1)S(1)}, bf16[512,512]{1,0:T(8,128)(2,1)}, u32[]{:S(2)}) copy-start(bf16[512,512]{1,0:T(8,128)(2,1)} %param.16) | copy-start | bytes 1572868
  2.5 1.2 %copy-start.5 = (bf16[256,512]{1,0:T(8,128)(2,1)S(1)}, bf16[256,512]{1,0:T(8,128)(2,1)}, u32[]{:S(2)}) copy-start(bf16[256,512]{1,0:T(8,128)(2,1)} %param.19) | copy-start | bytes 786436
  2.7 0.7 copy-start.9
  3.7 10.9 %copy-start.8 = (f32[128,128]{1,0:T(8,128)S(1)}, f32[128,128]{1,0:T(8,128)}, u32[]{:S(2)}) copy-start(f32[128,128]{1,0:T(8,128)} %param.14) | copy-start | bytes 196612
  3.7 10.9 %copy-start.10 = (s32[128]{0:T(128)S(1)}, s32[128]{0:T(128)}, u32[]{:S(2)}) copy-start(s32[128]{0:T(128)} %param.13) | copy-start | bytes 1540
  3.9 11.7 %copy-start.6 = (bf16[512,512]{1,0:T(8,128)(2,1)S(1)}, bf16[512,512]{1,0:T(8,128)(2,1)}, u32[]{:S(2)}) copy-start(bf16[512,512]{1,0:T(8,128)(2,1)} %param.17) | copy-start | bytes 1572868
  14.6 0.9 copy-start.3
  26.0 0.8 copy-start.4
  26.0 0.9 copy-start.2
  27.0 0.9 copy-start.1
  96.2 0.7 copy-start.11
where the time goes:
time: 99.2 us; the launch traced here: 98.7 us
  blocking collectives  82.3 us (83%)
  matrix products  6.91 us (7%)
  local copies, waits for them, and re-layouts  6.16 us (6%)
  between operations  1.7 us (2%)
  other arithmetic  1.61 us (2%)
    all_gather x4, blocking collectives, climb(): gathered = lax.all_gather(piece[None], 'leaf', axis=0, tiled=True)  36.8 us
    all_gather x4, blocking collectives, descend(): gathered = lax.all_gather(outgoing[None], 'leaf', axis=0, tiled=True)  31.9 us
    unnamed x1, blocking collectives  13.6 us
    unnamed x27, local copies, waits for them, and re-layouts  5.69 us
    dot_general x12, matrix products, across(): lax.dot_general(former, latter, (((1,), (1,)), ((), ())), preferred_eleme...  3.42 us
    dot_general x14, matrix products, plain_dot(): return jnp.dot(former, latter, preferred_element_type=jnp.float32)  3.11 us

commit v1 on v0

--- a/solution.py
+++ b/solution.py
@@ -3,6 +3,36 @@
 import jax.numpy as jnp
 from jax import lax
 from jax.sharding import PartitionSpec as P
+from jax.lax import axis_index, ppermute, psum
+
+
+def touch_the_vectors(my_tile, array_axis):
+    part_next = list(my_tile.shape[1:])
+    part_next[array_axis] *= my_tile.shape[0]
+    return jnp.moveaxis(my_tile, 0, array_axis).reshape(part_next)
+
+
+def apply_cells(x_in, dev_axis):
+    newest = psum(1, dev_axis)
+    z_new = axis_index(dev_axis)
+    h_now, b_next = (newest, z_new)
+    view_out, x_next = (x_in[None], 1)
+    while x_next < h_now:
+        block_last = range(h_now)
+        main = map(lambda kk: (kk, kk ^ x_next), block_last)
+        v1 = list(main)
+        frame_out = ppermute(view_out, dev_axis, v1)
+        reply = b_next & x_next == 0
+        taken_in = jnp.where(reply, view_out, frame_out)
+        moved = jnp.where(reply, frame_out, view_out)
+        view_out = jnp.concatenate([taken_in, moved])
+        x_next *= 2
+    return view_out
+
+
+def work_pieces_all(mine, in_array, k_dim=0):
+    z1 = apply_cells(mine, in_array)
+    return touch_the_vectors(z1, k_dim)
 
 
 def across(former, latter):
@@ -77,7 +107,7 @@
     for height in range(1, levels + 1):
         lowest = (height - 1) * block_size
         piece = jnp.stack([summed[:, lowest : lowest + block_size] for summed in contributions])
-        gathered = lax.all_gather(piece[None], "leaf", axis=0, tiled=True)
+        gathered = work_pieces_all(piece[None], "leaf")
         first = device >> height << height
         total = jnp.sum(lax.dynamic_slice_in_dim(gathered, first, 1 << height, 0), axis=0)
         owner = device % (1 << height) == 0

time: 99.2 us -> 83.4 us (0.84)
  blocking collectives: 82.3 us -> 46 us
  starting transfers between devices: 0 us -> 12.3 us
  waiting for transfers between devices: 0 us -> 8.26 us
    all_gather x4 -> x0, blocking collectives: 36.8 us -> none  [climb(): gathered = lax.all_gather(piece[None], 'leaf', axis=0, tiled=True)]
    ppermute x0 -> x8, starting transfers between devices: none -> 12.3 us  [apply_cells(): frame_out = ppermute(view_out, dev_axis, v1)]
    ppermute x0 -> x8, waiting for transfers between devices: none -> 8.26 us  [apply_cells(): frame_out = ppermute(view_out, dev_axis, v1)]
  transfers between devices with their start and end apart: 0 -> 8, of which waited for: 0 -> 6; matrix products, arithmetic and copies ran while one was open for 0% -> 4% of each run, Pallas kernels for 0% -> 0%
where the time goes in v1:
time: 83.4 us; the launch traced here: 83 us
  blocking collectives  46 us (55%)
  starting transfers between devices  12.3 us (15%)
  waiting for transfers between devices  8.26 us (10%)
  matrix products  6.92 us (8%)
  local copies, waits for them, and re-layouts  6.04 us (7%)
  other arithmetic  1.79 us (2%)
  between operations  1.74 us (2%)
    all_gather x4, blocking collectives, descend(): gathered = lax.all_gather(outgoing[None], 'leaf', axis=0, tiled=True)  32.4 us
    unnamed x1, blocking collectives  13.6 us
    ppermute x8, starting transfers between devices, apply_cells(): frame_out = ppermute(view_out, dev_axis, v1)  12.3 us
    ppermute x8, waiting for transfers between devices, apply_cells(): frame_out = ppermute(view_out, dev_axis, v1)  8.26 us
    unnamed x27, local copies, waits for them, and re-layouts  5.57 us
    dot_general x12, matrix products, across(): lax.dot_general(former, latter, (((1,), (1,)), ((), ())), preferred_eleme...  3.43 us
    dot_general x14, matrix products, plain_dot(): return jnp.dot(former, latter, preferred_element_type=jnp.float32)  3.11 us
  transfers between devices with their start and end apart: 8, of which 6 were waited for; matrix products, arithmetic and copies ran while one was open for 4% of the time, Pallas kernels for 0%

profile of v1, /device:TPU:0, one launch (start us, length us, event | category | flops | bytes accessed | tf_op | source)
XLA Modules:
  0.0 83.0 jit_solution(11813431986653702561)
XLA Ops:
  0.6 0.0 copy-start
  0.7 0.7 broadcast_subtract_fusion
  1.5 0.9 %fusion.196 = (bf16[128,128]{0,1:T(8,128)(2,1)S(1)}, f32[128,128]{0,1:T(8,128)S(1)}) fusion(bf16[512,512]{1,0:T(8,128)(2,1)} %param.16, f32[128,512]{0,1:T(8,128)S(1)} %fusion.15), kind=kOutput, calls=%fused_computation.237 | convolution fusion | flops 4227072 | bytes 229376 | tf_op jit(solution)/shard_map/dot_general | solution.py:39
  2.4 0.2 fusion.197
  2.5 0.2 convolution_subtract_fusion.5
  2.7 0.5 copy-done.9
  3.2 0.2 slice_reduce_fusion
  3.4 0.1 broadcast_bitcast_fusion.1
  3.5 0.2 convolution_multiply_fusion.1
  3.8 3.0 %collective-permute-start = (f32[1,1,1,128,128]{4,3,2,1,0:T(8,128)S(1)}, f32[1,1,1,128,128]{4,3,2,1,0:T(8,128)S(1)}, u32[]{:S(2)}, u32[]{:S(2)}) collective-permute-start(f32[1,1,1,128,128]{4,3,2,1,0:T(8,128)S(1)} %slice_bitcast_fusion.1), channel_id=1, source_target_pairs={{0,8},{8,0},{16,24},{24,16},{1,9},{9,1},{17,25},{25,17},{2,10},{10... | collective-permute-start | bytes 196616 | tf_op jit(solution)/shard_map/ppermute | solution.py:24
  6.8 0.4 convolution_bitcast_fusion
  7.2 0.2 fusion.187
  7.4 0.3 fusion.188
  7.8 0.4 fusion.191
  8.2 0.4 fusion.12
  8.5 0.6 copy-done.1
  9.1 0.2 convolution_multiply_fusion
  9.3 0.8 collective-permute-start.4
  10.1 0.1 broadcast_bitcast_fusion
  10.3 1.6 %collective-permute-start.1 = (f32[2,1,1,128,128]{4,3,2,1,0:T(8,128)S(1)}, f32[2,1,1,128,128]{4,3,2,1,0:T(8,128)S(1)}, u32[]{:S(2)}, u32[]{:S(2)}) collective-permute-start(f32[2,1,1,128,128]{4,3,2,1,0:T(8,128)S(1)} %pad_maximum_fusion.4), channel_id=1, source_target_pairs={{0,16},{8,24},{16,0},{24,8},{1,17},{9,25},{17,1},{25,9},{2,18},{10... | collective-permute-start | bytes 393224 | tf_op jit(solution)/shard_map/ppermute | solution.py:24
  11.9 1.8 %collective-permute-done.4 = f32[1,1,1,128,128]{4,3,2,1,0:T(8,128)S(1)} collective-permute-done((f32[1,1,1,128,128]{4,3,2,1,0:T(8,128)S(1)}, f32[1,1,1,128,128]{4,3,2,1,0:T(8,128)S(1)}, u32[]{:S(2)}, u32[]{:S(2)}) %collective-permute-start.4) | collective-permute-done | bytes 65568 | tf_op jit(solution)/shard_map/ppermute | solution.py:24
  13.7 1.6 %collective-permute-start.5 = (f32[2,1,1,128,128]{4,3,2,1,0:T(8,128)S(1)}, f32[2,1,1,128,128]{4,3,2,1,0:T(8,128)S(1)}, u32[]{:S(2)}, u32[]{:S(2)}) collective-permute-start(f32[2,1,1,128,128]{4,3,2,1,0:T(8,128)S(1)} %pad_maximum_fusion.6), channel_id=1, source_target_pairs={{0,16},{8,24},{16,0},{24,8},{1,17},{9,25},{17,1},{25,9},{2,18},{10... | collective-permute-start | bytes 393224 | tf_op jit(solution)/shard_map/ppermute | solution.py:24
  15.3 0.6 collective-permute-done.1
  15.9 2.9 %collective-permute-done.5 = f32[2,1,1,128,128]{4,3,2,1,0:T(8,128)S(1)} collective-permute-done((f32[2,1,1,128,128]{4,3,2,1,0:T(8,128)S(1)}, f32[2,1,1,128,128]{4,3,2,1,0:T(8,128)S(1)}, u32[]{:S(2)}, u32[]{:S(2)}) %collective-permute-start.5) | collective-permute-done | bytes 131104 | tf_op jit(solution)/shard_map/ppermute | solution.py:24
  18.8 0.1 fusion.23
  18.9 0.8 copy-done.5
  19.6 0.1 fusion.128
  19.7 0.0 copy-done.3
  19.8 0.1 fusion.96
  19.9 0.8 copy-done.2
  20.7 0.2 fusion.103
  20.9 0.8 collective-permute-start.6
  21.6 0.1 broadcast_bitcast_fusion.2
  21.7 0.7 copy-done.11
  22.4 0.6 dynamic-slice.2
  23.6 1.4 %collective-permute-start.2 = (f32[1,1,1,128,128]{4,3,2,1,0:T(8,128)S(1)}, f32[1,1,1,128,128]{4,3,2,1,0:T(8,128)S(1)}, u32[]{:S(2)}, u32[]{:S(2)}) collective-permute-start(f32[1,1,1,128,128]{4,3,2,1,0:T(8,128)S(1)} %get-tuple-element.32), channel_id=1, source_target_pairs={{0,8},{8,0},{16,24},{24,16},{1,9},{9,1},{17,25},{25,17},{2,10},{10... | collective-permute-start | bytes 196616 | tf_op jit(solution)/shard_map/ppermute | solution.py:24
  25.0 0.8 collective-permute-done.6
  25.8 1.6 %collective-permute-start.7 = (f32[2,1,1,128,128]{4,3,2,1,0:T(8,128)S(1)}, f32[2,1,1,128,128]{4,3,2,1,0:T(8,128)S(1)}, u32[]{:S(2)}, u32[]{:S(2)}) collective-permute-start(f32[2,1,1,128,128]{4,3,2,1,0:T(8,128)S(1)} %pad_maximum_fusion.7), channel_id=1, source_target_pairs={{0,16},{8,24},{16,0},{24,8},{1,17},{9,25},{17,1},{25,9},{2,18},{10... | collective-permute-start | bytes 393224 | tf_op jit(solution)/shard_map/ppermute | solution.py:24
  27.4 0.6 collective-permute-done.2
  28.0 1.6 %collective-permute-start.3 = (f32[2,1,1,128,128]{4,3,2,1,0:T(8,128)S(1)}, f32[2,1,1,128,128]{4,3,2,1,0:T(8,128)S(1)}, u32[]{:S(2)}, u32[]{:S(2)}) collective-permute-start(f32[2,1,1,128,128]{4,3,2,1,0:T(8,128)S(1)} %pad_maximum_fusion.5), channel_id=1, source_target_pairs={{0,16},{8,24},{16,0},{24,8},{1,17},{9,25},{17,1},{25,9},{2,18},{10... | collective-permute-start | bytes 393224 | tf_op jit(solution)/shard_map/ppermute | solution.py:24
  29.6 1.7 %collective-permute-done.7 = f32[2,1,1,128,128]{4,3,2,1,0:T(8,128)S(1)} collective-permute-done((f32[2,1,1,128,128]{4,3,2,1,0:T(8,128)S(1)}, f32[2,1,1,128,128]{4,3,2,1,0:T(8,128)S(1)}, u32[]{:S(2)}, u32[]{:S(2)}) %collective-permute-start.7) | collective-permute-done | bytes 131104 | tf_op jit(solution)/shard_map/ppermute | solution.py:24
  31.3 0.1 fusion.129
  31.4 0.1 fusion.4
  31.6 9.0 %all-gather.2 = bf16[512,128]{1,0:T(8,128)(2,1)S(1)} all-gather(bf16[128,128]{1,0:T(8,128)(2,1)S(1)} %fusion.4), channel_id=4, replica_groups=mesh['leaf'=4,'src'=8] {'leaf'}, dimensions={0}, use_global_device_ids=true | all-gather | bytes 163840 | tf_op jit(solution)/shard_map/all_gather | solution.py:127
  40.6 0.1 fusion.5
  40.7 7.3 %all-gather.3 = bf16[512,128]{1,0:T(8,128)(2,1)S(1)} all-gather(bf16[128,128]{1,0:T(8,128)(2,1)S(1)} %fusion.5), channel_id=5, replica_groups=mesh['leaf'=4,'src'=8] {'leaf'}, dimensions={0}, use_global_device_ids=true | all-gather | bytes 163840 | tf_op jit(solution)/shard_map/all_gather | solution.py:127
  48.1 0.3 convolution_subtract_fusion
  48.4 0.2 fusion.198
  48.6 0.3 convolution_convert_fusion.1
  48.9 8.6 %all-gather = bf16[512,128]{1,0:T(8,128)(2,1)S(1)} all-gather(bf16[128,128]{1,0:T(8,128)(2,1)S(1)} %convolution_convert_fusion.1), channel_id=2, replica_groups=mesh['leaf'=4,'src'=8] {'leaf'}, dimensions={0}, use_global_device_ids=true | all-gather | bytes 163840 | tf_op jit(solution)/shard_map/all_gather | solution.py:127
  57.5 0.3 convolution_convert_fusion
  57.8 7.5 %all-gather.1 = bf16[512,128]{1,0:T(8,128)(2,1)S(1)} all-gather(bf16[128,128]{1,0:T(8,128)(2,1)S(1)} %convolution_convert_fusion), channel_id=3, replica_groups=mesh['leaf'=4,'src'=8] {'leaf'}, dimensions={0}, use_global_device_ids=true | all-gather | bytes 163840 | tf_op jit(solution)/shard_map/all_gather | solution.py:127
  65.3 0.2 convolution_subtract_fusion.1
  65.6 0.1 fusion.200
  65.7 0.3 fusion.201
  66.0 0.3 fusion.204
  66.3 0.3 fusion.9
  66.6 0.2 fusion.199
  66.8 0.2 convolution_subtract_fusion.8
  67.1 0.1 multiply_reduce_fusion
  67.2 0.8 %copy.21 = f32[128,512]{1,0:T(8,128)} copy(f32[128,512]{0,1:T(8,128)S(1)} %get-tuple-element.17) | data formatting | bytes 524288
  68.0 0.8 %copy.22 = f32[128,512]{1,0:T(8,128)} copy(f32[128,512]{0,1:T(8,128)S(1)} %get-tuple-element.18) | data formatting | bytes 524288
  68.9 13.6 %all-reduce.2 = f32[512]{0:T(512)S(1)} all-reduce(f32[512]{0:T(512)S(1)} %get-tuple-element.16), channel_id=6, replica_groups=mesh['leaf'=4,'src'=8] {'src'}, use_global_device_ids=true, to_apply=%region_7.8.clone | all-reduce | flops 512 | bytes 4096
  82.5 0.6 dynamic-slice_multiply_fusion
  (48 shorter events, 0.4 us)
Async XLA Ops:
  0.6 2.9 %copy-start = (bf16[256,512]{1,0:T(8,128)(2,1)S(1)}, bf16[256,512]{1,0:T(8,128)(2,1)}, u32[]{:S(2)}) copy-start(bf16[256,512]{1,0:T(8,128)(2,1)} %param.19) | copy-start | bytes 786436
  0.6 1.7 %copy-start.7 = (bf16[512,512]{1,0:T(8,128)(2,1)S(1)}, bf16[512,512]{1,0:T(8,128)(2,1)}, u32[]{:S(2)}) copy-start(bf16[512,512]{1,0:T(8,128)(2,1)} %param.16) | copy-start | bytes 1572868
  2.5 0.7 copy-start.9
  3.5 3.9 %copy-start.6 = (bf16[512,512]{1,0:T(8,128)(2,1)S(1)}, bf16[512,512]{1,0:T(8,128)(2,1)}, u32[]{:S(2)}) copy-start(bf16[512,512]{1,0:T(8,128)(2,1)} %param.17) | copy-start | bytes 1572868
  3.8 3.1 %copy-start.8 = (f32[128,128]{1,0:T(8,128)S(1)}, f32[128,128]{1,0:T(8,128)}, u32[]{:S(2)}) copy-start(f32[128,128]{1,0:T(8,128)} %param.14) | copy-start | bytes 196612
  3.8 3.0 %copy-start.10 = (s32[128]{0:T(128)S(1)}, s32[128]{0:T(128)}, u32[]{:S(2)}) copy-start(s32[128]{0:T(128)} %param.13) | copy-start | bytes 1540
  3.8 3.4 %copy-start.4 = (bf16[4,128,128]{2,1,0:T(8,128)(2,1)S(1)}, bf16[4,128,128]{2,1,0:T(8,128)(2,1)}, u32[]{:S(2)}) copy-start(bf16[4,128,128]{2,1,0:T(8,128)(2,1)} %param.18) | copy-start | bytes 393220
  3.8 6.4 %collective-permute-start = (f32[1,1,1,128,128]{4,3,2,1,0:T(8,128)S(1)}, f32[1,1,1,128,128]{4,3,2,1,0:T(8,128)S(1)}, u32[]{:S(2)}, u32[]{:S(2)}) collective-permute-start(f32[1,1,1,128,128]{4,3,2,1,0:T(8,128)S(1)} %slice_bitcast_fusion.1), channel_id=1, source_target_pairs={{0,8},{8,0},{16,24},{24,16},{1,9},{9,1},{17,25},{25,17},{2,10},{10... | collective-permute-start | bytes 196616 | tf_op jit(solution)/shard_map/ppermute | solution.py:24
  8.1 1.0 %copy-start.1 = (bf16[512,256]{1,0:T(8,128)(2,1)S(1)}, bf16[512,256]{1,0:T(8,128)(2,1)}, u32[]{:S(2)}) copy-start(bf16[512,256]{1,0:T(8,128)(2,1)} %param.20) | copy-start | bytes 786436
  9.3 4.3 %collective-permute-start.4 = (f32[1,1,1,128,128]{4,3,2,1,0:T(8,128)S(1)}, f32[1,1,1,128,128]{4,3,2,1,0:T(8,128)S(1)}, u32[]{:S(2)}, u32[]{:S(2)}) collective-permute-start(f32[1,1,1,128,128]{4,3,2,1,0:T(8,128)S(1)} %slice_bitcast_fusion), channel_id=1, source_target_pairs={{0,8},{8,0},{16,24},{24,16},{1,9},{9,1},{17,25},{25,17},{2,10},{10... | collective-permute-start | bytes 196616 | tf_op jit(solution)/shard_map/ppermute | solution.py:24
  10.3 5.6 %collective-permute-start.1 = (f32[2,1,1,128,128]{4,3,2,1,0:T(8,128)S(1)}, f32[2,1,1,128,128]{4,3,2,1,0:T(8,128)S(1)}, u32[]{:S(2)}, u32[]{:S(2)}) collective-permute-start(f32[2,1,1,128,128]{4,3,2,1,0:T(8,128)S(1)} %pad_maximum_fusion.4), channel_id=1, source_target_pairs={{0,16},{8,24},{16,0},{24,8},{1,17},{9,25},{17,1},{25,9},{2,18},{10... | collective-permute-start | bytes 393224 | tf_op jit(solution)/shard_map/ppermute | solution.py:24
  13.7 5.0 %collective-permute-start.5 = (f32[2,1,1,128,128]{4,3,2,1,0:T(8,128)S(1)}, f32[2,1,1,128,128]{4,3,2,1,0:T(8,128)S(1)}, u32[]{:S(2)}, u32[]{:S(2)}) collective-permute-start(f32[2,1,1,128,128]{4,3,2,1,0:T(8,128)S(1)} %pad_maximum_fusion.6), channel_id=1, source_target_pairs={{0,16},{8,24},{16,0},{24,8},{1,17},{9,25},{17,1},{25,9},{2,18},{10... | collective-permute-start | bytes 393224 | tf_op jit(solution)/shard_map/ppermute | solution.py:24
  18.8 0.8 %copy-start.5 = (bf16[2,128,128]{2,1,0:T(8,128)(2,1)S(1)}, bf16[2,128,128]{2,1,0:T(8,128)(2,1)}, u32[]{:S(2)}) copy-start(bf16[2,128,128]{2,1,0:T(8,128)(2,1)} %param.21) | copy-start | bytes 196612
  18.8 0.9 %copy-start.3 = (bf16[2,128,256]{2,1,0:T(8,128)(2,1)S(1)}, bf16[2,128,256]{2,1,0:T(8,128)(2,1)}, u32[]{:S(2)}) copy-start(bf16[2,128,256]{2,1,0:T(8,128)(2,1)} %param.23) | copy-start | bytes 393220
  19.8 0.9 %copy-start.2 = (bf16[2,256,128]{2,1,0:T(8,128)(2,1)S(1)}, bf16[2,256,128]{2,1,0:T(8,128)(2,1)}, u32[]{:S(2)}) copy-start(bf16[2,256,128]{2,1,0:T(8,128)(2,1)} %param.22) | copy-start | bytes 393220
  20.9 4.9 %collective-permute-start.6 = (f32[1,1,1,128,128]{4,3,2,1,0:T(8,128)S(1)}, f32[1,1,1,128,128]{4,3,2,1,0:T(8,128)S(1)}, u32[]{:S(2)}, u32[]{:S(2)}) collective-permute-start(f32[1,1,1,128,128]{4,3,2,1,0:T(8,128)S(1)} %get-tuple-element.31), channel_id=1, source_target_pairs={{0,8},{8,0},{16,24},{24,16},{1,9},{9,1},{17,25},{25,17},{2,10},{10... | collective-permute-start | bytes 196616 | tf_op jit(solution)/shard_map/ppermute | solution.py:24
  21.7 0.7 copy-start.11
  23.6 4.3 %collective-permute-start.2 = (f32[1,1,1,128,128]{4,3,2,1,0:T(8,128)S(1)}, f32[1,1,1,128,128]{4,3,2,1,0:T(8,128)S(1)}, u32[]{:S(2)}, u32[]{:S(2)}) collective-permute-start(f32[1,1,1,128,128]{4,3,2,1,0:T(8,128)S(1)} %get-tuple-element.32), channel_id=1, source_target_pairs={{0,8},{8,0},{16,24},{24,16},{1,9},{9,1},{17,25},{25,17},{2,10},{10... | collective-permute-start | bytes 196616 | tf_op jit(solution)/shard_map/ppermute | solution.py:24
  25.8 5.5 %collective-permute-start.7 = (f32[2,1,1,128,128]{4,3,2,1,0:T(8,128)S(1)}, f32[2,1,1,128,128]{4,3,2,1,0:T(8,128)S(1)}, u32[]{:S(2)}, u32[]{:S(2)}) collective-permute-start(f32[2,1,1,128,128]{4,3,2,1,0:T(8,128)S(1)} %pad_maximum_fusion.7), channel_id=1, source_target_pairs={{0,16},{8,24},{16,0},{24,8},{1,17},{9,25},{17,1},{25,9},{2,18},{10... | collective-permute-start | bytes 393224 | tf_op jit(solution)/shard_map/ppermute | solution.py:24
  28.0 20.6 %collective-permute-start.3 = (f32[2,1,1,128,128]{4,3,2,1,0:T(8,128)S(1)}, f32[2,1,1,128,128]{4,3,2,1,0:T(8,128)S(1)}, u32[]{:S(2)}, u32[]{:S(2)}) collective-permute-start(f32[2,1,1,128,128]{4,3,2,1,0:T(8,128)S(1)} %pad_maximum_fusion.5), channel_id=1, source_target_pairs={{0,16},{8,24},{16,0},{24,8},{1,17},{9,25},{17,1},{25,9},{2,18},{10... | collective-permute-start | bytes 393224 | tf_op jit(solution)/shard_map/ppermute | solution.py:24
